TPU v7x, 32 devices: a whole 2x2x4 slice. The times are simulated.
32 devices in a mesh: lvl: 4 (over y, x), prow: 4 (over z), pcol: 2 (over core).
Axes of the slice: x: 2, y: 2, z: 4, core: 2. Of those that a mesh axis runs over, the one named last changes fastest.
Arguments:
- rhs: float32 [4, 2, 1024, 256], P('lvl', 'pcol'), may hold values from -6 to 6
- diag_inverse: bfloat16 [4, 2, 1024, 1024], P('lvl', 'pcol', 'prow'), may hold values from -0.1875 to 0.1875
- off_tiles: bfloat16 [4, 2, 32, 32, 1024], P('lvl', 'pcol', 'prow'), may hold values from -0.625 to 0.625
- panel_super: int32 [4, 2, 8], P('lvl', 'pcol'), may hold values from 0 to 7, as said below
- off_device: int32 [4, 2, 32], P('lvl', 'pcol', 'prow'), may hold values from 0 to 7, as said below
- off_block: int32 [4, 2, 32], P('lvl', 'pcol', 'prow'), may hold values from 0 to 47, as said below
- offdiag_block_panel: int32 [4, 2, 32], P('lvl', 'pcol', 'prow'), may hold values from 0 to 7
Outputs:
- solution: float32 [4, 2, 1024, 256], P('lvl', 'pcol', 'prow')
- outer: float32 [4, 2, 512, 256], P('lvl', 'pcol')
Inputs may be any that keep to these rules, and one draw needn't show every extreme that they name: `panel_super`: within a group ids start at 0 and rise by 0 or 1 from panel to panel; panels of one id form one supernode. `off_device`: one device sends at most 2 block rows to any one target group; some group receives 2 from every device. `off_block`: A block under 1024 / 32 (a window row) goes only to a group on a higher level than the sender's; the others are rows above the window.
All inputs are finite; a program needn't handle non-finite values.
Results may differ from a plain program's by a relative error of at most 0.0055.
Values may be sent and summed in bfloat16 or wider, within the bound.
No kernel may reach another device: no remote copies, remote signals or barrier semaphores. Data moves between devices by JAX's collectives and lax.ppermute only.
A program may use at most 64 MiB of HBM per device.

v0:
```python
import jax
import jax.numpy as jnp
from jax import lax
from jax.sharding import PartitionSpec as P

CAP = 2
ABOVE = 512
NT = 48


def per_device(
    rhs, diag_inverse, off_tiles, panel_super, off_device, off_block, offdiag_block_panel
):
    levels = lax.axis_size("lvl")
    col_groups = lax.axis_size("pcol")
    groups = levels * col_groups
    level_index = lax.axis_index("lvl")
    row_index = lax.axis_index("prow")
    width = rhs.shape[2]
    columns_all = rhs.shape[3]
    row_count = diag_inverse.shape[2]
    tile_count = off_tiles.shape[2]
    block_rows = off_tiles.shape[3]
    panels = panel_super[0, 0]
    panel_cols = width // panels.shape[0]
    col_super = jnp.repeat(panels, panel_cols)
    row_ids = row_index * row_count + jnp.arange(row_count, dtype=jnp.int32)
    row_super = jnp.take(col_super, row_ids)
    inverse = jnp.where(
        row_super[:, None] == col_super[None, :], diag_inverse[0, 0], jnp.zeros((), jnp.bfloat16)
    )
    tile_supernode = jnp.take(panels, offdiag_block_panel[0, 0])
    tiles_used = jnp.where(
        col_super[None, None, :] == tile_supernode[:, None, None],
        off_tiles[0, 0],
        jnp.zeros((), jnp.bfloat16),
    )
    tiles_used = tiles_used.reshape(tile_count * block_rows, width)
    target = off_device[0, 0]
    target_block = off_block[0, 0]
    tile_ids = jnp.arange(tile_count, dtype=jnp.int32)
    earlier = (target[:, None] == target[None, :]) & (tile_ids[:, None] > tile_ids[None, :])
    position = jnp.sum(earlier.astype(jnp.int32), axis=1)
    slot_index = target * CAP + position
    slot_total = groups * CAP
    match = slot_index[None, :] == jnp.arange(slot_total, dtype=jnp.int32)[:, None]
    filled = jnp.any(match, axis=1)
    chosen = jnp.sum(jnp.where(match, tile_ids[None, :], 0), axis=1)
    slot_block = jnp.where(filled, jnp.take(target_block, chosen), -1)
    slot_level = jnp.arange(slot_total, dtype=jnp.int32) // (col_groups * CAP)
    col_blocks = 1
    block_cols = columns_all // col_blocks
    right = rhs[0, 0]
    solved = jnp.zeros((row_count, columns_all), jnp.float32)
    outer = jnp.zeros((ABOVE, columns_all), jnp.float32)
    block_numbers = jnp.arange(NT, dtype=jnp.int32)
    for section in range(levels + col_blocks - 1):
        my_block = section - level_index
        active = (my_block >= 0) & (my_block < col_blocks)
        right_part = right
        solved_rows = jnp.dot(
            inverse, right_part.astype(jnp.bfloat16), preferred_element_type=jnp.float32
        )
        previous = solved
        solved = jnp.where(active, solved_rows, previous)
        updates = jnp.dot(
            tiles_used,
            lax.all_gather(solved_rows.astype(jnp.bfloat16), "prow", axis=0, tiled=True),
            preferred_element_type=jnp.float32,
        )
        updates = updates.astype(jnp.bfloat16).reshape(tile_count, block_rows, block_cols)
        padded = jnp.concatenate(
            [updates, jnp.zeros((1, block_rows, block_cols), jnp.bfloat16)], axis=0
        )
        sending = jnp.take(padded, jnp.where(filled & active, chosen, tile_count), axis=0)
        send_block = jnp.where(active, slot_block, -1)
        incoming_block_rows, received_block = (
            lax.all_to_all(sending, ("lvl", "pcol"), split_axis=0, concat_axis=0, tiled=True),
            lax.all_to_all(send_block, ("lvl", "pcol"), split_axis=0, concat_axis=0, tiled=True),
        )
        from_level = slot_level == section
        choosing_mask = (
            (received_block[:, None] == block_numbers[None, :]) & from_level[:, None]
        ).astype(jnp.bfloat16)
        block_fragments = jnp.einsum(
            "at,apz->tpz", choosing_mask, incoming_block_rows, preferred_element_type=jnp.float32
        )
        summed = block_fragments
        summed = summed.reshape(NT * block_rows, columns_all)
        summed = lax.psum(summed, "prow")
        right = right - summed[:width]
        outer = outer + summed[width:]
    return (solved[None, None], outer[None, None])


def solution(mesh):
    placed = (
        P("lvl", "pcol", None, None),
        P("lvl", "pcol", "prow", None),
        P("lvl", "pcol", "prow", None, None),
        P("lvl", "pcol", None),
        P("lvl", "pcol", "prow"),
        P("lvl", "pcol", "prow"),
        P("lvl", "pcol", "prow"),
    )
    return jax.shard_map(
        per_device,
        mesh=mesh,
        in_specs=placed,
        out_specs=(P("lvl", "pcol", "prow", None), P("lvl", "pcol", None, None)),
        check_vma=False,
    )
```

profile of v0, /device:TPU:0, one launch (start us, length us, event | category | flops | bytes accessed | tf_op | source)
XLA Modules:
  0.0 433.2 jit_solution(8528554265465169059)
XLA Ops:
  9.2 1.3 gather_fusion.1
  11.8 5.2 %all-to-all-start = ((s32[8,2,1]{1,2,0:T(1,128)}), s32[8,2,1]{1,2,0:T(1,128)S(1)}, u32[]{:S(2)}, u32[]{:S(2)}) async-start(s32[8,2,1]{1,2,0:T(1,128)} %bitcast.9), calls=%async_computation | async-start | bytes 8192 | tf_op jit(solution)/shard_map/all_to_all | solution.py:79
  19.1 1.4 gather_fusion
  21.7 16.6 %all_gather.12 = bf16[1024,256]{1,0:T(8,128)(2,1)S(1)} all-gather(bf16[256,256]{1,0:T(8,128)(2,1)S(1)} %get-tuple-element.24), channel_id=1, replica_groups=mesh['lvl'=4,'prow'=4,'pcol'=2] {'prow'}, dimensions={0}, use_global_device_ids=true | all-gather | bytes 655360 | tf_op jit(solution)/shard_map/all_gather | solution.py:68
  40.0 3.8 all-to-all-start.1
  45.1 5.6 %all-to-all-done.1 = bf16[16,32,256]{2,1,0:T(8,128)(2,1)S(1)} async-done(((bf16[16,32,256]{2,1,0:T(8,128)(2,1)}), bf16[16,32,256]{2,1,0:T(8,128)(2,1)S(1)}, u32[]{:S(2)}, u32[]{:S(2)}) %all-to-all-start.1) | async-done | bytes 262176 | tf_op jit(solution)/shard_map/all_to_all | solution.py:78
  51.2 2.1 copy.31
  53.3 3.3 all-to-all-start.2
  56.6 65.5 %all-reduce.9.cloned.1.call-done = f32[1536,256]{1,0:T(8,128)} async-done(((f32[1536,256]{1,0:T(8,128)}), f32[1536,256]{1,0:T(8,128)}) %all-reduce.9.cloned.1.call-update) | async-done | bytes 1572880 | tf_op jit(solution)/shard_map/psum | solution.py:90
  122.2 2.3 fusion.51
  124.5 15.8 %all_gather.13 = bf16[1024,256]{1,0:T(8,128)(2,1)S(1)} all-gather(bf16[256,256]{1,0:T(8,128)(2,1)S(1)} %get-tuple-element.26), channel_id=1, replica_groups=mesh['lvl'=4,'prow'=4,'pcol'=2] {'prow'}, dimensions={0}, use_global_device_ids=true | all-gather | bytes 655360 | tf_op jit(solution)/shard_map/all_gather | solution.py:68
  142.0 3.4 all-to-all-start.3
  146.2 6.1 %all-to-all-done.3 = bf16[16,32,256]{2,1,0:T(8,128)(2,1)S(1)} async-done(((bf16[16,32,256]{2,1,0:T(8,128)(2,1)}), bf16[16,32,256]{2,1,0:T(8,128)(2,1)S(1)}, u32[]{:S(2)}, u32[]{:S(2)}) %all-to-all-start.3) | async-done | bytes 262176 | tf_op jit(solution)/shard_map/all_to_all | solution.py:78
  152.8 2.1 copy.34
  154.9 3.5 all-to-all-start.4
  158.4 63.7 %all-reduce.11.cloned.1.call-done = f32[1536,256]{1,0:T(8,128)} async-done(((f32[1536,256]{1,0:T(8,128)}), f32[1536,256]{1,0:T(8,128)}) %all-reduce.11.cloned.1.call-update) | async-done | bytes 1572880 | tf_op jit(solution)/shard_map/psum | solution.py:90
  222.0 2.6 fusion.52
  224.6 15.8 %all_gather.14 = bf16[1024,256]{1,0:T(8,128)(2,1)S(1)} all-gather(bf16[256,256]{1,0:T(8,128)(2,1)S(1)} %get-tuple-element.28), channel_id=1, replica_groups=mesh['lvl'=4,'prow'=4,'pcol'=2] {'prow'}, dimensions={0}, use_global_device_ids=true | all-gather | bytes 655360 | tf_op jit(solution)/shard_map/all_gather | solution.py:68
  240.8 1.3 gather_fusion.5
  242.1 1.7 broadcast_select_fusion.1
  243.8 3.4 all-to-all-start.5
  248.0 6.1 %all-to-all-done.5 = bf16[16,32,256]{2,1,0:T(8,128)(2,1)S(1)} async-done(((bf16[16,32,256]{2,1,0:T(8,128)(2,1)}), bf16[16,32,256]{2,1,0:T(8,128)(2,1)S(1)}, u32[]{:S(2)}, u32[]{:S(2)}) %all-to-all-start.5) | async-done | bytes 262176 | tf_op jit(solution)/shard_map/all_to_all | solution.py:78
  254.6 2.1 copy.37
  256.7 3.5 all-to-all-start.6
  260.2 63.7 %all-reduce.13.cloned.1.call-done = f32[1536,256]{1,0:T(8,128)} async-done(((f32[1536,256]{1,0:T(8,128)}), f32[1536,256]{1,0:T(8,128)}) %all-reduce.13.cloned.1.call-update) | async-done | bytes 1572880 | tf_op jit(solution)/shard_map/psum | solution.py:90
  323.8 2.9 fusion.49
  326.8 15.8 %all_gather.15 = bf16[1024,256]{1,0:T(8,128)(2,1)S(1)} all-gather(bf16[256,256]{1,0:T(8,128)(2,1)S(1)} %get-tuple-element.13), channel_id=1, replica_groups=mesh['lvl'=4,'prow'=4,'pcol'=2] {'prow'}, dimensions={0}, use_global_device_ids=true | all-gather | bytes 655360 | tf_op jit(solution)/shard_map/all_gather | solution.py:68
  344.3 3.4 all-to-all-start.7
  348.5 6.1 %all-to-all-done.7 = bf16[16,32,256]{2,1,0:T(8,128)(2,1)S(1)} async-done(((bf16[16,32,256]{2,1,0:T(8,128)(2,1)}), bf16[16,32,256]{2,1,0:T(8,128)(2,1)S(1)}, u32[]{:S(2)}, u32[]{:S(2)}) %all-to-all-start.7) | async-done | bytes 262176 | tf_op jit(solution)/shard_map/all_to_all | solution.py:78
  355.1 2.1 copy.40
  357.2 67.2 %all-reduce.15.cloned.1.call-done = f32[1536,256]{1,0:T(8,128)} async-done(((f32[1536,256]{1,0:T(8,128)}), f32[1536,256]{1,0:T(8,128)}) %all-reduce.15.cloned.1.call-update) | async-done | bytes 1572880 | tf_op jit(solution)/shard_map/psum | solution.py:90
  424.3 2.3 fusion.6
  (82 shorter events, 17.5 us)
Async XLA Ops:
  7.2 10.5 %copy-start = (s32[1,1,8]{2,1,0:T(1,128)S(1)}, s32[1,1,8]{2,1,0:T(1,128)}, u32[]{:S(2)}) copy-start(s32[1,1,8]{2,1,0:T(1,128)} %param.12) | copy-start | bytes 100
  7.2 13.4 %copy-start.3 = (bf16[1,1,256,1024]{3,2,1,0:T(8,128)(2,1)S(1)}, bf16[1,1,256,1024]{3,2,1,0:T(8,128)(2,1)}, u32[]{:S(2)}) copy-start(bf16[1,1,256,1024]{3,2,1,0:T(8,128)(2,1)} %param.10) | copy-start | bytes 1572868
  7.2 13.4 %copy-start.1 = (f32[1,1,1024,256]{3,2,1,0:T(8,128)S(1)}, f32[1,1,1024,256]{3,2,1,0:T(8,128)}, u32[]{:S(2)}) copy-start(f32[1,1,1024,256]{3,2,1,0:T(8,128)} %param.9) | copy-start | bytes 3145732
  11.8 28.2 %all-to-all-start = ((s32[8,2,1]{1,2,0:T(1,128)}), s32[8,2,1]{1,2,0:T(1,128)S(1)}, u32[]{:S(2)}, u32[]{:S(2)}) async-start(s32[8,2,1]{1,2,0:T(1,128)} %bitcast.9), calls=%async_computation | async-start | bytes 8192 | tf_op jit(solution)/shard_map/all_to_all | solution.py:79
  20.5 17.8 %copy-start.5 = (bf16[1,1,8,32,1024]{4,3,2,1,0:T(8,128)(2,1)S(1)}, bf16[1,1,8,32,1024]{4,3,2,1,0:T(8,128)(2,1)}, u32[]{:S(2)}) copy-start(bf16[1,1,8,32,1024]{4,3,2,1,0:T(8,128)(2,1)} %param.11) | copy-start | bytes 1572868
  40.0 10.7 %all-to-all-start.1 = ((bf16[16,32,256]{2,1,0:T(8,128)(2,1)}), bf16[16,32,256]{2,1,0:T(8,128)(2,1)S(1)}, u32[]{:S(2)}, u32[]{:S(2)}) async-start(bf16[16,32,256]{2,1,0:T(8,128)(2,1)} %broadcast_select_fusion.3), calls=%async_computation.1 | async-start | bytes 524288 | tf_op jit(solution)/shard_map/all_to_all | solution.py:78
  43.8 78.4 %all-reduce.9.cloned.1.call-start = ((), (), s32[]{:S(2)}) async-start(), calls=%async_computation.8 | async-start | bytes 3145728 | tf_op jit(solution)/shard_map/psum | solution.py:90
  53.3 88.7 %all-to-all-start.2 = ((s32[8,2,1]{1,2,0:T(1,128)}), s32[8,2,1]{1,2,0:T(1,128)S(1)}, u32[]{:S(2)}, u32[]{:S(2)}) async-start(s32[8,2,1]{1,2,0:T(1,128)} %bitcast.20), calls=%async_computation.2 | async-start | bytes 8192 | tf_op jit(solution)/shard_map/all_to_all | solution.py:79
  142.0 10.3 %all-to-all-start.3 = ((bf16[16,32,256]{2,1,0:T(8,128)(2,1)}), bf16[16,32,256]{2,1,0:T(8,128)(2,1)S(1)}, u32[]{:S(2)}, u32[]{:S(2)}) async-start(bf16[16,32,256]{2,1,0:T(8,128)(2,1)} %broadcast_select_fusion.2), calls=%async_computation.3 | async-start | bytes 524288 | tf_op jit(solution)/shard_map/all_to_all | solution.py:78
  145.4 76.6 %all-reduce.11.cloned.1.call-start = ((), (), s32[]{:S(2)}) async-start(), calls=%async_computation.9 | async-start | bytes 3145728 | tf_op jit(solution)/shard_map/psum | solution.py:90
  154.9 67.2 %copy-start.2 = (f32[1536,256]{1,0:T(8,128)S(1)}, f32[1536,256]{1,0:T(8,128)}, u32[]{:S(2)}) copy-start(f32[1536,256]{1,0:T(8,128)} %all-reduce.9.cloned.1.call-done) | copy-start | bytes 4718596
  154.9 88.9 %all-to-all-start.4 = ((s32[8,2,1]{1,2,0:T(1,128)}), s32[8,2,1]{1,2,0:T(1,128)S(1)}, u32[]{:S(2)}, u32[]{:S(2)}) async-start(s32[8,2,1]{1,2,0:T(1,128)} %bitcast.24), calls=%async_computation.4 | async-start | bytes 8192 | tf_op jit(solution)/shard_map/all_to_all | solution.py:79
  243.8 10.3 %all-to-all-start.5 = ((bf16[16,32,256]{2,1,0:T(8,128)(2,1)}), bf16[16,32,256]{2,1,0:T(8,128)(2,1)S(1)}, u32[]{:S(2)}, u32[]{:S(2)}) async-start(bf16[16,32,256]{2,1,0:T(8,128)(2,1)} %broadcast_select_fusion.1), calls=%async_computation.5 | async-start | bytes 524288 | tf_op jit(solution)/shard_map/all_to_all | solution.py:78
  247.2 76.6 %all-reduce.13.cloned.1.call-start = ((), (), s32[]{:S(2)}) async-start(), calls=%async_computation.10 | async-start | bytes 3145728 | tf_op jit(solution)/shard_map/psum | solution.py:90
  256.6 67.2 %copy-start.4 = (f32[256,256]{1,0:T(8,128)S(1)}, f32[256,256]{1,0:T(8,128)}, u32[]{:S(2)}) copy-start(f32[256,256]{1,0:T(8,128)} %get-tuple-element.25) | copy-start | bytes 786436
  256.7 87.6 %all-to-all-start.6 = ((s32[8,2,1]{1,2,0:T(1,128)}), s32[8,2,1]{1,2,0:T(1,128)S(1)}, u32[]{:S(2)}, u32[]{:S(2)}) async-start(s32[8,2,1]{1,2,0:T(1,128)} %bitcast.29), calls=%async_computation.6 | async-start | bytes 8192 | tf_op jit(solution)/shard_map/all_to_all | solution.py:79
  344.3 10.3 %all-to-all-start.7 = ((bf16[16,32,256]{2,1,0:T(8,128)(2,1)}), bf16[16,32,256]{2,1,0:T(8,128)(2,1)S(1)}, u32[]{:S(2)}, u32[]{:S(2)}) async-start(bf16[16,32,256]{2,1,0:T(8,128)(2,1)} %broadcast_select_fusion), calls=%async_computation.7 | async-start | bytes 524288 | tf_op jit(solution)/shard_map/all_to_all | solution.py:78
  347.7 76.6 %all-reduce.15.cloned.1.call-start = ((), (), s32[]{:S(2)}) async-start(), calls=%async_computation.11 | async-start | bytes 3145728 | tf_op jit(solution)/shard_map/psum | solution.py:90
Sparse Core Ops, SparseCore 0:
  53.4 68.6 all-reduce.8
  155.0 66.9 all-reduce.10
  256.8 66.9 all-reduce.12
  357.3 66.9 all-reduce.14
where the time goes:
time: 434 us; the launch traced here: 433 us
  waiting for transfers between devices  284 us (65%)
  blocking collectives  64.1 us (15%)
  starting transfers between devices  29.6 us (7%)
  local copies, waits for them, and re-layouts  15.8 us (4%)
  between operations  14.1 us (3%)
  other arithmetic  13.5 us (3%)
  matrix products  12 us (3%)
    psum x4, waiting for transfers between devices, per_device(): summed = lax.psum(summed, 'prow')  260 us
    all_gather x4, blocking collectives, per_device(): lax.all_gather(solved_rows.astype(jnp.bfloat16), 'prow', axis=0, tiled=True)  64.1 us
    all_to_all x4, waiting for transfers between devices, per_device(): lax.all_to_all(sending, ('lvl', 'pcol'), split_axis=0, concat_axis=0, til...  23.9 us
    all_to_all x4, starting transfers between devices, per_device(): lax.all_to_all(send_block, ('lvl', 'pcol'), split_axis=0, concat_axis=0,...  15.4 us
    all_to_all x4, starting transfers between devices, per_device(): lax.all_to_all(sending, ('lvl', 'pcol'), split_axis=0, concat_axis=0, til...  14 us
    dot_general x4, matrix products, per_device(): jnp.dot(inverse, right_part.astype(jnp.bfloat16), preferred_element_type=...  8.92 us
  transfers between devices with their start and end apart: 12, of which 8 were waited for; matrix products, arithmetic and copies ran while one was open for 6% of the time, Pallas kernels for 0%

commit v1 on v0

--- a/solution.py
+++ b/solution.py
@@ -87,7 +87,7 @@
         )
         summed = block_fragments
         summed = summed.reshape(NT * block_rows, columns_all)
-        summed = lax.psum(summed, "prow")
+        summed = jnp.sum(lax.all_gather(summed, "prow"), axis=0)
         right = right - summed[:width]
         outer = outer + summed[width:]
     return (solved[None, None], outer[None, None])

time: 434 us -> 635 us (1.46)
  waiting for transfers between devices: 284 us -> 465 us
  other arithmetic: 13.5 us -> 30.6 us
    all_gather x0 -> x4, waiting for transfers between devices: none -> 441 us  [per_device(): summed = jnp.sum(lax.all_gather(summed, 'prow'), axis=0)]
    psum x4 -> x0, waiting for transfers between devices: 260 us -> none  [per_device(): summed = lax.psum(summed, 'prow')]
    reduce_sum x0 -> x4, other arithmetic: none -> 16.1 us  [per_device(): summed = jnp.sum(lax.all_gather(summed, 'prow'), axis=0)]
where the time goes in v1:
time: 635 us; the launch traced here: 633 us
  waiting for transfers between devices  465 us (73%)
  blocking collectives  65.3 us (10%)
  other arithmetic  30.6 us (5%)
  starting transfers between devices  29.7 us (5%)
  local copies, waits for them, and re-layouts  16.5 us (3%)
  between operations  14.1 us (2%)
  matrix products  11.8 us (2%)
    all_gather x4, waiting for transfers between devices, per_device(): summed = jnp.sum(lax.all_gather(summed, 'prow'), axis=0)  441 us
    all_gather x4, blocking collectives, per_device(): lax.all_gather(solved_rows.astype(jnp.bfloat16), 'prow', axis=0, tiled=True)  65.3 us
    all_to_all x4, waiting for transfers between devices, per_device(): lax.all_to_all(sending, ('lvl', 'pcol'), split_axis=0, concat_axis=0, til...  24 us
    reduce_sum x4, other arithmetic, per_device(): summed = jnp.sum(lax.all_gather(summed, 'prow'), axis=0)  16.1 us
    all_to_all x4, starting transfers between devices, per_device(): lax.all_to_all(send_block, ('lvl', 'pcol'), split_axis=0, concat_axis=0,...  14.9 us
    all_to_all x4, starting transfers between devices, per_device(): lax.all_to_all(sending, ('lvl', 'pcol'), split_axis=0, concat_axis=0, til...  14.7 us
  transfers between devices with their start and end apart: 12, of which 8 were waited for; matrix products, arithmetic and copies ran while one was open for 6% of the time, Pallas kernels for 0%

profile of v1, /device:TPU:0, one launch (start us, length us, event | category | flops | bytes accessed | tf_op | source)
XLA Modules:
  0.0 633.5 jit_solution(7282015135312317026)
XLA Ops:
  11.8 5.2 all-to-all-start
  21.6 16.6 %all_gather.24 = bf16[1024,256]{1,0:T(8,128)(2,1)S(1)} all-gather(bf16[256,256]{1,0:T(8,128)(2,1)S(1)} %get-tuple-element.24), channel_id=1, replica_groups=mesh['lvl'=4,'prow'=4,'pcol'=2] {'prow'}, dimensions={0}, use_global_device_ids=true | all-gather | bytes 655360 | tf_op jit(solution)/shard_map/all_gather | solution.py:68
  40.0 3.8 all-to-all-start.1
  45.1 5.6 all-to-all-done.1
  51.2 2.1 copy.31
  53.3 3.2 all-to-all-start.2
  56.5 111.8 %all-gather.5.cloned.1.call-done = f32[4,1536,256]{2,1,0:T(8,128)} async-done(((f32[1,1536,256]{2,1,0:T(8,128)}), f32[4,1536,256]{2,1,0:T(8,128)}) %all-gather.5.cloned.1.call-update) | async-done | bytes 6291472 | tf_op jit(solution)/shard_map/all_gather | solution.py:90
  168.4 3.5 reduce_sum.62
  171.9 2.2 fusion.51
  174.0 16.2 %all_gather.26 = bf16[1024,256]{1,0:T(8,128)(2,1)S(1)} all-gather(bf16[256,256]{1,0:T(8,128)(2,1)S(1)} %get-tuple-element.26), channel_id=1, replica_groups=mesh['lvl'=4,'prow'=4,'pcol'=2] {'prow'}, dimensions={0}, use_global_device_ids=true | all-gather | bytes 655360 | tf_op jit(solution)/shard_map/all_gather | solution.py:68
  193.6 3.6 all-to-all-start.3
  198.0 6.1 all-to-all-done.3
  204.6 2.1 copy.34
  206.7 3.3 all-to-all-start.4
  210.0 108.7 %all-gather.7.cloned.1.call-done = f32[4,1536,256]{2,1,0:T(8,128)} async-done(((f32[1,1536,256]{2,1,0:T(8,128)}), f32[4,1536,256]{2,1,0:T(8,128)}) %all-gather.7.cloned.1.call-update) | async-done | bytes 6291472 | tf_op jit(solution)/shard_map/all_gather | solution.py:90
  318.7 4.5 reduce_sum.63
  323.3 2.5 fusion.52
  325.8 16.2 %all_gather.28 = bf16[1024,256]{1,0:T(8,128)(2,1)S(1)} all-gather(bf16[256,256]{1,0:T(8,128)(2,1)S(1)} %get-tuple-element.28), channel_id=1, replica_groups=mesh['lvl'=4,'prow'=4,'pcol'=2] {'prow'}, dimensions={0}, use_global_device_ids=true | all-gather | bytes 655360 | tf_op jit(solution)/shard_map/all_gather | solution.py:68
  345.4 3.6 all-to-all-start.5
  349.8 6.1 all-to-all-done.5
  356.4 2.1 copy.37
  358.6 3.3 all-to-all-start.6
  361.9 108.7 %all-gather.9.cloned.1.call-done = f32[4,1536,256]{2,1,0:T(8,128)} async-done(((f32[1,1536,256]{2,1,0:T(8,128)}), f32[4,1536,256]{2,1,0:T(8,128)}) %all-gather.9.cloned.1.call-update) | async-done | bytes 6291472 | tf_op jit(solution)/shard_map/all_gather | solution.py:90
  470.6 4.6 reduce_sum.64
  475.2 2.9 fusion.49
  478.2 16.3 %all_gather.30 = bf16[1024,256]{1,0:T(8,128)(2,1)S(1)} all-gather(bf16[256,256]{1,0:T(8,128)(2,1)S(1)} %get-tuple-element.13), channel_id=1, replica_groups=mesh['lvl'=4,'prow'=4,'pcol'=2] {'prow'}, dimensions={0}, use_global_device_ids=true | all-gather | bytes 655360 | tf_op jit(solution)/shard_map/all_gather | solution.py:68
  496.2 3.6 all-to-all-start.7
  500.5 6.1 all-to-all-done.7
  507.2 2.1 copy.40
  509.3 112.0 %all-gather.11.cloned.1.call-done = f32[4,1536,256]{2,1,0:T(8,128)} async-done(((f32[1,1536,256]{2,1,0:T(8,128)}), f32[4,1536,256]{2,1,0:T(8,128)}) %all-gather.11.cloned.1.call-update) | async-done | bytes 6291472 | tf_op jit(solution)/shard_map/all_gather | solution.py:90
  621.3 3.5 reduce_sum.65
  624.7 2.2 fusion.6
  (84 shorter events, 24.9 us)
Async XLA Ops:
  7.2 10.5 %copy-start = (s32[1,1,8]{2,1,0:T(1,128)S(1)}, s32[1,1,8]{2,1,0:T(1,128)}, u32[]{:S(2)}) copy-start(s32[1,1,8]{2,1,0:T(1,128)} %param.12) | copy-start | bytes 100
  7.2 13.4 %copy-start.2 = (bf16[1,1,256,1024]{3,2,1,0:T(8,128)(2,1)S(1)}, bf16[1,1,256,1024]{3,2,1,0:T(8,128)(2,1)}, u32[]{:S(2)}) copy-start(bf16[1,1,256,1024]{3,2,1,0:T(8,128)(2,1)} %param.10) | copy-start | bytes 1572868
  7.2 13.4 %copy-start.1 = (f32[1,1,1024,256]{3,2,1,0:T(8,128)S(1)}, f32[1,1,1024,256]{3,2,1,0:T(8,128)}, u32[]{:S(2)}) copy-start(f32[1,1,1024,256]{3,2,1,0:T(8,128)} %param.9) | copy-start | bytes 3145732
  11.8 28.2 %all-to-all-start = ((s32[8,2,1]{1,2,0:T(1,128)}), s32[8,2,1]{1,2,0:T(1,128)S(1)}, u32[]{:S(2)}, u32[]{:S(2)}) async-start(s32[8,2,1]{1,2,0:T(1,128)} %bitcast.9), calls=%async_computation | async-start | bytes 8192 | tf_op jit(solution)/shard_map/all_to_all | solution.py:79
  20.5 17.8 %copy-start.4 = (bf16[1,1,8,32,1024]{4,3,2,1,0:T(8,128)(2,1)S(1)}, bf16[1,1,8,32,1024]{4,3,2,1,0:T(8,128)(2,1)}, u32[]{:S(2)}) copy-start(bf16[1,1,8,32,1024]{4,3,2,1,0:T(8,128)(2,1)} %param.11) | copy-start | bytes 1572868
  40.0 10.7 %all-to-all-start.1 = ((bf16[16,32,256]{2,1,0:T(8,128)(2,1)}), bf16[16,32,256]{2,1,0:T(8,128)(2,1)S(1)}, u32[]{:S(2)}, u32[]{:S(2)}) async-start(bf16[16,32,256]{2,1,0:T(8,128)(2,1)} %broadcast_select_fusion.3), calls=%async_computation.1 | async-start | bytes 524288 | tf_op jit(solution)/shard_map/all_to_all | solution.py:78
  43.8 124.6 %all-gather.5.cloned.1.call-start = ((), (), s32[]{:S(2)}) async-start(), calls=%async_computation.8 | async-start | bytes 7864320 | tf_op jit(solution)/shard_map/all_gather | solution.py:90
  53.3 140.3 %all-to-all-start.2 = ((s32[8,2,1]{1,2,0:T(1,128)}), s32[8,2,1]{1,2,0:T(1,128)S(1)}, u32[]{:S(2)}, u32[]{:S(2)}) async-start(s32[8,2,1]{1,2,0:T(1,128)} %bitcast.20), calls=%async_computation.2 | async-start | bytes 8192 | tf_op jit(solution)/shard_map/all_to_all | solution.py:79
  193.6 10.6 %all-to-all-start.3 = ((bf16[16,32,256]{2,1,0:T(8,128)(2,1)}), bf16[16,32,256]{2,1,0:T(8,128)(2,1)S(1)}, u32[]{:S(2)}, u32[]{:S(2)}) async-start(bf16[16,32,256]{2,1,0:T(8,128)(2,1)} %broadcast_select_fusion.2), calls=%async_computation.3 | async-start | bytes 524288 | tf_op jit(solution)/shard_map/all_to_all | solution.py:78
  197.2 121.5 %all-gather.7.cloned.1.call-start = ((), (), s32[]{:S(2)}) async-start(), calls=%async_computation.9 | async-start | bytes 7864320 | tf_op jit(solution)/shard_map/all_gather | solution.py:90
  206.7 138.7 %all-to-all-start.4 = ((s32[8,2,1]{1,2,0:T(1,128)}), s32[8,2,1]{1,2,0:T(1,128)S(1)}, u32[]{:S(2)}, u32[]{:S(2)}) async-start(s32[8,2,1]{1,2,0:T(1,128)} %bitcast.24), calls=%async_computation.4 | async-start | bytes 8192 | tf_op jit(solution)/shard_map/all_to_all | solution.py:79
  345.4 10.6 %all-to-all-start.5 = ((bf16[16,32,256]{2,1,0:T(8,128)(2,1)}), bf16[16,32,256]{2,1,0:T(8,128)(2,1)S(1)}, u32[]{:S(2)}, u32[]{:S(2)}) async-start(bf16[16,32,256]{2,1,0:T(8,128)(2,1)} %broadcast_select_fusion.1), calls=%async_computation.5 | async-start | bytes 524288 | tf_op jit(solution)/shard_map/all_to_all | solution.py:78
  349.0 121.6 %all-gather.9.cloned.1.call-start = ((), (), s32[]{:S(2)}) async-start(), calls=%async_computation.10 | async-start | bytes 7864320 | tf_op jit(solution)/shard_map/all_gather | solution.py:90
  358.6 137.6 %all-to-all-start.6 = ((s32[8,2,1]{1,2,0:T(1,128)}), s32[8,2,1]{1,2,0:T(1,128)S(1)}, u32[]{:S(2)}, u32[]{:S(2)}) async-start(s32[8,2,1]{1,2,0:T(1,128)} %bitcast.29), calls=%async_computation.6 | async-start | bytes 8192 | tf_op jit(solution)/shard_map/all_to_all | solution.py:79
  361.9 113.3 %copy-start.3 = (f32[256,256]{1,0:T(8,128)S(1)}, f32[256,256]{1,0:T(8,128)}, u32[]{:S(2)}) copy-start(f32[256,256]{1,0:T(8,128)} %get-tuple-element.25) | copy-start | bytes 786436
  496.2 10.5 %all-to-all-start.7 = ((bf16[16,32,256]{2,1,0:T(8,128)(2,1)}), bf16[16,32,256]{2,1,0:T(8,128)(2,1)S(1)}, u32[]{:S(2)}, u32[]{:S(2)}) async-start(bf16[16,32,256]{2,1,0:T(8,128)(2,1)} %broadcast_select_fusion), calls=%async_computation.7 | async-start | bytes 524288 | tf_op jit(solution)/shard_map/all_to_all | solution.py:78
  499.7 121.5 %all-gather.11.cloned.1.call-start = ((), (), s32[]{:S(2)}) async-start(), calls=%async_computation.11 | async-start | bytes 7864320 | tf_op jit(solution)/shard_map/all_gather | solution.py:90
Sparse Core Ops, SparseCore 0:
  53.4 114.9 all-gather.4
  206.8 111.8 all-gather.6
  358.7 111.8 all-gather.8
  509.4 111.8 all-gather.10
